TPU v7x, 32 devices: a whole 2x2x4 slice. The times are simulated.
32 devices in a mesh: groups: 2 (over y), ctx: 4 (over z), head: 4 (over x, core).
Axes of the slice: x: 2, y: 2, z: 4, core: 2. Of those that a mesh axis runs over, the one named last changes fastest.
Arguments:
- hidden_in: bfloat16 [2048, 4096], P(('groups', 'ctx'), 'head'), parts along dimension 0, may hold values from -6 to 6
- norm_gain: bfloat16 [4096], P('head'), may hold values from 0.099609375 to 1.8984375
- w_query: bfloat16 [4096, 2048], P('ctx', 'head'), may hold values from -8 to 8
- w_key: bfloat16 [4096, 512], P('ctx', 'head'), may hold values from -8 to 8
- w_value: bfloat16 [4096, 512], P('ctx', 'head'), may hold values from -0.09375 to 0.09375
- w_out: bfloat16 [2048, 4096], P('head', 'ctx'), may hold values from -3 to 3
- session_ids: int32 [2048], P('groups'), parts along dimension 0, may hold values from 0 to 3, never falling along the last dimension, each value on 1 to 512 neighbouring positions
- block_anchor: int32 [16], P('groups'), parts along dimension 0, may hold values from 0 to 7, each once
Outputs:
- block_update: bfloat16 [2048, 4096], P(('groups', 'ctx'), 'head'), parts along dimension 0
There are 2 independent parts, one for each index of `groups`. A program takes and returns all parts, laid end to end along the dimension named above; an argument that names none is the same for every part. Nothing has to cross between parts.
Inputs may be any that keep to these rules, and one draw needn't show every extreme that they name: `session_ids`: session numbers never fall along the contiguous order; 4 sessions, each of 1 to 512 tokens, one of exactly 512. `block_anchor`: each of the 8 blocks appears once.
All inputs are finite; a program needn't handle non-finite values.
Results may differ from a plain program's by a relative error of at most 0.0095.
The roundings to bfloat16 on the way count: a program that leaves them out, or rounds other values in their place, can miss the bound.
Values may be sent and summed in bfloat16 or wider, within the bound.
No kernel may reach another device: no remote copies, remote signals or barrier semaphores. Data moves between devices by JAX's collectives and lax.ppermute only.
A program may use at most 64 MiB of HBM per device.

v0:
```python
import math

import jax
import jax.numpy as jnp
from jax import lax
from jax.sharding import PartitionSpec as P

HD = 128
GROUP = 4
BLOCK = 128


norm_epsilon = 1e-05
rotary_base = 500000.0
masked_score = -1e30


def passed_along(block, axis, distance):
    devices = range(lax.axis_size(axis))
    route = [((i - distance) % len(devices), i) for i in devices]
    return lax.ppermute(block, axis, route)


def session_starts(session_ids):
    length = session_ids.shape[0]
    indices = jnp.arange(length, dtype=jnp.int32)
    fresh = jnp.concatenate([jnp.ones((1,), dtype=jnp.bool_), session_ids[1:] != session_ids[:-1]])
    return lax.cummax(jnp.where(fresh, indices, 0), axis=0)


def rotary(vectors, position):
    half_dim = vectors.shape[-1] // 2
    ladder = jnp.arange(half_dim, dtype=jnp.float32) * (2.0 / vectors.shape[-1])
    frequency = jnp.exp(-ladder * math.log(rotary_base))
    angles = position.astype(jnp.float32).reshape((-1,) + (1,) * (vectors.ndim - 1)) * frequency
    cosine = jnp.cos(angles)
    sines = jnp.sin(angles)
    first_half = vectors[..., :half_dim]
    second_half = vectors[..., half_dim:]
    return jnp.concatenate(
        [first_half * cosine - second_half * sines, second_half * cosine + first_half * sines],
        axis=-1,
    )


def attend_core(
    carry_state, query_heads, query_pos, query_seg, key_heads, value_heads, key_pos, key_seg
):
    row_max, row_sum, mixed_sum = carry_state
    scores = jnp.einsum(
        "qagd,kad->qagk", query_heads, key_heads, preferred_element_type=jnp.float32
    ) * (1.0 / math.sqrt(query_heads.shape[-1]))
    allowed = ((query_seg[:, None] == key_seg[None, :]) & (key_pos[None, :] <= query_pos[:, None]))[
        :, None, None, :
    ]
    new_max = jnp.maximum(row_max, jnp.max(jnp.where(allowed, scores, masked_score), axis=-1))
    weights = jnp.where(allowed, jnp.exp(scores - new_max[..., None]), 0.0)
    rescale = jnp.exp(row_max - new_max)
    row_sum = row_sum * rescale + jnp.sum(weights, axis=-1)
    mixed_sum = mixed_sum * rescale[..., None] + jnp.einsum(
        "qagk,kad->qagd",
        weights.astype(jnp.bfloat16),
        value_heads,
        preferred_element_type=jnp.float32,
    )
    return (new_max, row_sum, mixed_sum)


def per_device(hidden_in, norm_gain, w_query, w_key, w_value, w_out, session_ids, block_anchor):
    whole, gain_full = (
        lax.all_gather(hidden_in, "head", axis=1, tiled=True),
        lax.all_gather(norm_gain, "head", axis=0, tiled=True),
    )
    tok_rows = whole.shape[0]
    cycle_size = lax.axis_size("ctx")
    cycle_index = lax.axis_index("ctx")
    per_shard = tok_rows // BLOCK
    starts = session_starts(session_ids)
    seg_table = session_ids.reshape(-1, BLOCK)
    start_table = starts.reshape(-1, BLOCK)
    offsets = jnp.arange(BLOCK, dtype=jnp.int32)

    def token_info(owner):
        blocks_here = lax.dynamic_slice_in_dim(block_anchor, owner * per_shard, per_shard)
        contiguous = (blocks_here[:, None] * BLOCK + offsets[None, :]).reshape(-1)
        session = jnp.take(seg_table, blocks_here, axis=0).reshape(-1)
        position = contiguous - jnp.take(start_table, blocks_here, axis=0).reshape(-1)
        return (contiguous, session, position)

    wide = whole.astype(jnp.float32)
    normed = (
        wide
        * lax.rsqrt(jnp.mean(wide * wide, axis=-1, keepdims=True) + norm_epsilon)
        * gain_full.astype(jnp.float32)
    ).astype(jnp.bfloat16)
    key_cols = w_key.shape[1]
    kv_local = key_cols // HD
    pieces = (
        lax.all_gather(w_query, "ctx", axis=0, tiled=True),
        lax.all_gather(w_key, "ctx", axis=0, tiled=True),
        lax.all_gather(w_value, "ctx", axis=0, tiled=True),
    )
    query_raw, key_raw, value_raw = tuple(
        (jnp.dot(normed, weight_rows, preferred_element_type=jnp.float32) for weight_rows in pieces)
    )
    my_pos, my_seg, my_place = token_info(cycle_index)
    query_heads = rotary(query_raw.reshape(tok_rows, kv_local, GROUP, HD), my_place).astype(
        jnp.bfloat16
    )
    key_heads = rotary(key_raw.reshape(tok_rows, kv_local, HD), my_place).astype(jnp.bfloat16)
    value_heads = value_raw.astype(jnp.bfloat16).reshape(tok_rows, kv_local, HD)

    def attend(current_state, kv_stack, source):
        key_pos, key_seg, unused_place = token_info(source)
        return attend_core(
            current_state, query_heads, my_pos, my_seg, kv_stack[0], kv_stack[1], key_pos, key_seg
        )

    carry_state = (
        jnp.full((tok_rows, kv_local, GROUP), masked_score, jnp.float32),
        jnp.zeros((tok_rows, kv_local, GROUP), jnp.float32),
        jnp.zeros((tok_rows, kv_local, GROUP, HD), jnp.float32),
    )
    own_stack = jnp.stack([key_heads, value_heads])
    carry_state = attend(carry_state, own_stack, cycle_index)

    def cycle_turn(turn_index, loop_carry):
        current_state, moving = loop_carry
        moving = passed_along(moving, "ctx", 1)
        current_state = attend(current_state, moving, (cycle_index - turn_index) % cycle_size)
        return (current_state, moving)

    carry_state, unused_stack = lax.fori_loop(1, cycle_size, cycle_turn, (carry_state, own_stack))
    final_max, row_sum, mixed_sum = carry_state
    attended = (mixed_sum / row_sum[..., None]).astype(jnp.bfloat16).reshape(tok_rows, -1)
    terms = jnp.dot(
        attended,
        lax.all_gather(w_out, "ctx", axis=1, tiled=True),
        preferred_element_type=jnp.float32,
    )
    return lax.psum_scatter(terms.astype(jnp.bfloat16), "head", scatter_dimension=1, tiled=True)


def solution(mesh):
    in_specs = (
        P(("groups", "ctx"), "head"),
        P("head"),
        P("ctx", "head"),
        P("ctx", "head"),
        P("ctx", "head"),
        P("head", "ctx"),
        P("groups"),
        P("groups"),
    )
    out_specs = P(("groups", "ctx"), "head")
    return jax.shard_map(
        per_device, mesh=mesh, in_specs=in_specs, out_specs=out_specs, check_vma=False
    )
```

profile of v0, /device:TPU:2, one launch (start us, length us, event | category | flops | bytes accessed | tf_op | source)
XLA Modules:
  0.0 299.4 jit_solution(423023249203372490)
XLA Ops:
  6.5 0.7 all-gather.6.cloned.1.call-update
  7.3 0.7 all-gather.8.cloned.1.call-update
  8.1 0.7 all-gather.12.cloned.1.call-update
  10.0 0.7 broadcast_multiply_fusion.1
  10.7 0.7 compare_and_fusion.3
  11.4 0.8 slice_compare_fusion
  12.3 1.2 gather_fusion.1
  13.7 5.3 %all_gather.19 = bf16[4096]{0:T(1024)(128)(2,1)S(1)} all-gather(bf16[1024]{0:T(1024)(128)(2,1)} %param.13), channel_id=1, replica_groups=mesh['groups'=2,'ctx'=4,'head'=4] {'head'}, dimensions={0}, use_global_device_ids=true | all-gather | bytes 10240 | tf_op jit(solution)/shard_map/all_gather | solution.py:72
  19.7 0.6 gather_fusion.2
  21.0 10.6 %all-gather.6.cloned.1.call-done = bf16[256,4096]{1,0:T(8,128)(2,1)} async-done(((bf16[256,1024]{1,0:T(8,128)(2,1)}), bf16[256,4096]{1,0:T(8,128)(2,1)}) %all-gather.6.cloned.1.call-update) | async-done | bytes 2097168 | tf_op jit(solution)/shard_map/all_gather | solution.py:71
  31.6 2.2 fusion.17
  33.8 28.5 %all-gather.8.cloned.1.call-done = bf16[4096,128]{1,0:T(8,128)(2,1)} async-done(((bf16[1024,128]{1,0:T(8,128)(2,1)}), bf16[4096,128]{1,0:T(8,128)(2,1)}) %all-gather.8.cloned.1.call-update) | async-done | bytes 1048592 | tf_op jit(solution)/shard_map/all_gather | solution.py:100
  62.3 2.8 convolution_bitcast_fusion.2
  65.5 25.8 %all-gather.12.cloned.1.call-done = bf16[4096,128]{1,0:T(8,128)(2,1)} async-done(((bf16[1024,128]{1,0:T(8,128)(2,1)}), bf16[4096,128]{1,0:T(8,128)(2,1)}) %all-gather.12.cloned.1.call-update) | async-done | bytes 1048592 | tf_op jit(solution)/shard_map/all_gather | solution.py:101
  91.3 2.2 convolution_convert_fusion.1
  93.6 79.2 %all-gather.10.cloned.1.call-done = bf16[4096,512]{1,0:T(8,128)(2,1)} async-done(((bf16[1024,512]{1,0:T(8,128)(2,1)}), bf16[4096,512]{1,0:T(8,128)(2,1)}) %all-gather.10.cloned.1.call-update) | async-done | bytes 4194320 | tf_op jit(solution)/shard_map/all_gather | solution.py:99
  172.9 3.5 %fusion.49 = f32[256,512]{1,0:T(8,128)S(1)} fusion(bf16[4096,512]{1,0:T(8,128)(2,1)} %all-gather.10.cloned.1.call-done, bf16[256,4096]{1,0:T(8,128)(2,1)S(1)} %copy-done, f32[4096]{0:T(1024)S(1)} %convert_element_type.65, f32[256]{0:T(256)S(1)} %add_rsqrt_fusion), kind=kOutput, calls=%fused_computation.101 | convolution fusion | flops 1077936128 | bytes 6833152 | tf_op jit(solution)/shard_map/dot_general | solution.py:104
  178.4 30.9 %while.22 = (s32[]{:T(128)}, f32[256,1,4]{0,2,1:T(4,128)S(1)}, f32[256,1,4]{0,2,1:T(4,128)S(1)}, f32[256,1,4,128]{3,0,2,1:T(8,128)S(1)}, bf16[2,256,1,128]{3,1,2...) while((s32[]{:T(128)}, f32[256,1,4]{0,2,1:T(4,128)S(1)}, ...), condition=%wide.region_8.10_spmd.clone, body=%wide.region_5.9_spmd.clone.sunk | while | flops 137040672 | bytes 5716408 | solution.py:133
  179.6 5.9 %collective-permute-done = bf16[2,256,1,128]{3,1,2,0:T(8,128)(2,1)S(1)} collective-permute-done((bf16[2,256,1,128]{3,1,2,0:T(8,128)(2,1)S(1)}, bf16[2,256,1,128]{3,1,2,0:T(8,128)(2,1)S(1)}, u32[]{:S(2)}, u32[]{:S(2)}) %collective-permute-start) | collective-permute-done | bytes 131104 | tf_op jit(solution)/shard_map/while/body/eval_jaxpr/ppermute | solution.py:21
  187.7 9.2 %collective-permute-done = bf16[2,256,1,128]{3,1,2,0:T(8,128)(2,1)S(1)} collective-permute-done((bf16[2,256,1,128]{3,1,2,0:T(8,128)(2,1)S(1)}, bf16[2,256,1,128]{3,1,2,0:T(8,128)(2,1)S(1)}, u32[]{:S(2)}, u32[]{:S(2)}) %collective-permute-start) | collective-permute-done | bytes 131104 | tf_op jit(solution)/shard_map/while/body/eval_jaxpr/ppermute | solution.py:21
  199.2 9.0 %collective-permute-done = bf16[2,256,1,128]{3,1,2,0:T(8,128)(2,1)S(1)} collective-permute-done((bf16[2,256,1,128]{3,1,2,0:T(8,128)(2,1)S(1)}, bf16[2,256,1,128]{3,1,2,0:T(8,128)(2,1)S(1)}, u32[]{:S(2)}, u32[]{:S(2)}) %collective-permute-start) | collective-permute-done | bytes 131104 | tf_op jit(solution)/shard_map/while/body/eval_jaxpr/ppermute | solution.py:21
  209.6 49.6 %all-gather.14.cloned.1.call-done = bf16[512,4096]{1,0:T(8,128)(2,1)} async-done(((bf16[512,1024]{1,0:T(8,128)(2,1)}), bf16[512,4096]{1,0:T(8,128)(2,1)}) %all-gather.14.cloned.1.call-update) | async-done | bytes 4194320 | tf_op jit(solution)/shard_map/all_gather | solution.py:138
  259.2 4.8 %convolution_convert_fusion = bf16[256,4096]{1,0:T(8,128)(2,1)} fusion(bf16[256,512]{0,1:T(8,128)(2,1)S(1)} %bitcast.132, bf16[512,4096]{1,0:T(8,128)(2,1)} %all-gather.14.cloned.1.call-done), kind=kOutput, calls=%fused_computation.36 | convolution fusion | flops 1074790400 | bytes 6553600 | tf_op jit(solution)/shard_map/dot_general | solution.py:136
  264.0 28.5 %reduce-scatter.2.cloned.1.call-done = bf16[256,1024]{1,0:T(8,128)(2,1)} async-done(((bf16[256,4096]{1,0:T(8,128)(2,1)}), bf16[256,1024]{1,0:T(8,128)(2,1)}) %reduce-scatter.2.cloned.1.call-update) | async-done | bytes 524304 | tf_op jit(solution)/shard_map/reduce_scatter | solution.py:141
  (91 shorter events, 12.0 us)
Async XLA Ops:
  6.5 25.1 %all-gather.6.cloned.1.call-start = ((), (), s32[]{:S(2)}) async-start(), calls=%async_computation.1 | async-start | bytes 2621440 | tf_op jit(solution)/shard_map/all_gather | solution.py:71
  7.3 55.0 %all-gather.8.cloned.1.call-start = ((), (), s32[]{:S(2)}) async-start(), calls=%async_computation.2 | async-start | bytes 1310720 | tf_op jit(solution)/shard_map/all_gather | solution.py:100
  8.0 83.3 %all-gather.12.cloned.1.call-start = ((), (), s32[]{:S(2)}) async-start(), calls=%async_computation.4 | async-start | bytes 1310720 | tf_op jit(solution)/shard_map/all_gather | solution.py:101
  8.7 164.1 %all-gather.10.cloned.1.call-start = ((), (), s32[]{:S(2)}) async-start(), calls=%async_computation.3 | async-start | bytes 5242880 | tf_op jit(solution)/shard_map/all_gather | solution.py:99
  9.3 249.9 %all-gather.14.cloned.1.call-start = ((), (), s32[]{:S(2)}) async-start(), calls=%async_computation.5 | async-start | bytes 5242880 | tf_op jit(solution)/shard_map/all_gather | solution.py:138
  9.9 282.6 %reduce-scatter.2.cloned.1.call-start = ((), (), s32[]{:S(2)}) async-start(), calls=%async_computation.6 | async-start | bytes 2621440 | tf_op jit(solution)/shard_map/reduce_scatter | solution.py:141
  31.6 59.7 %copy-start = (bf16[256,4096]{1,0:T(8,128)(2,1)S(1)}, bf16[256,4096]{1,0:T(8,128)(2,1)}, u32[]{:S(2)}) copy-start(bf16[256,4096]{1,0:T(8,128)(2,1)} %all-gather.6.cloned.1.call-done) | copy-start | bytes 6291460
  176.9 1.6 copy-start.1
  176.9 1.6 copy-start.2
  178.4 7.1 %collective-permute-start = (bf16[2,256,1,128]{3,1,2,0:T(8,128)(2,1)S(1)}, bf16[2,256,1,128]{3,1,2,0:T(8,128)(2,1)S(1)}, u32[]{:S(2)}, u32[]{:S(2)}) collective-permute-start(bf16[2,256,1,128]{3,1,2,0:T(8,128)(2,1)S(1)} %get-tuple-element.504), channel_id=1, source_target_pairs={{12,0},{0,4},{4,8},{8,12},{13,1},{1,5},{5,9},{9,13},{14,2},{2,6},{... | collective-permute-start | bytes 393224 | tf_op jit(solution)/shard_map/while/body/eval_jaxpr/ppermute | solution.py:21
  186.6 10.3 %collective-permute-start = (bf16[2,256,1,128]{3,1,2,0:T(8,128)(2,1)S(1)}, bf16[2,256,1,128]{3,1,2,0:T(8,128)(2,1)S(1)}, u32[]{:S(2)}, u32[]{:S(2)}) collective-permute-start(bf16[2,256,1,128]{3,1,2,0:T(8,128)(2,1)S(1)} %get-tuple-element.504), channel_id=1, source_target_pairs={{12,0},{0,4},{4,8},{8,12},{13,1},{1,5},{5,9},{9,13},{14,2},{2,6},{... | collective-permute-start | bytes 393224 | tf_op jit(solution)/shard_map/while/body/eval_jaxpr/ppermute | solution.py:21
  198.1 10.1 %collective-permute-start = (bf16[2,256,1,128]{3,1,2,0:T(8,128)(2,1)S(1)}, bf16[2,256,1,128]{3,1,2,0:T(8,128)(2,1)S(1)}, u32[]{:S(2)}, u32[]{:S(2)}) collective-permute-start(bf16[2,256,1,128]{3,1,2,0:T(8,128)(2,1)S(1)} %get-tuple-element.504), channel_id=1, source_target_pairs={{12,0},{0,4},{4,8},{8,12},{13,1},{1,5},{5,9},{9,13},{14,2},{2,6},{... | collective-permute-start | bytes 393224 | tf_op jit(solution)/shard_map/while/body/eval_jaxpr/ppermute | solution.py:21
Sparse Core Ops, SparseCore 0:
  8.9 22.6 all-gather.5
  33.2 29.0 all-gather.7
  63.9 27.3 all-gather.11
  92.7 80.1 all-gather.9
  174.3 84.8 all-gather.13
  264.1 28.3 reduce-scatter.1
where the time goes:
time: 302 us; the launch traced here: 299 us
  waiting for transfers between devices  250 us (83%)
  matrix products  16.6 us (5%)
  between operations  13.7 us (5%)
  other arithmetic  8.91 us (3%)
  blocking collectives  5.31 us (2%)
  local copies, waits for them, and re-layouts  4.74 us (2%)
    all_gather x1, waiting for transfers between devices, per_device(): lax.all_gather(w_query, 'ctx', axis=0, tiled=True)  79.2 us
    all_gather x1, waiting for transfers between devices, per_device(): lax.all_gather(w_out, 'ctx', axis=1, tiled=True)  49.6 us
    reduce_scatter x1, waiting for transfers between devices, per_device(): lax.psum_scatter(terms.astype(jnp.bfloat16), 'head', scatter_dimension=1,...  28.5 us
    all_gather x1, waiting for transfers between devices, per_device(): lax.all_gather(w_key, 'ctx', axis=0, tiled=True)  28.5 us
    all_gather x1, waiting for transfers between devices, per_device(): lax.all_gather(w_value, 'ctx', axis=0, tiled=True)  25.8 us
    ppermute x3, waiting for transfers between devices, passed_along(): return lax.ppermute(block, axis, route)  24.2 us
    all_gather x1, waiting for transfers between devices, per_device(): lax.all_gather(hidden_in, 'head', axis=1, tiled=True)  10.6 us
    dot_general x3, matrix products, per_device(): jnp.dot(normed, weight_rows, preferred_element_type=jnp.float32)  8.48 us
  transfers between devices with their start and end apart: 9, of which 9 were waited for; matrix products, arithmetic and copies ran while one was open for 8% of the time, Pallas kernels for 0%

commit v1 on v0

--- a/solution.py
+++ b/solution.py
@@ -66,7 +66,7 @@
     return (new_max, row_sum, mixed_sum)
 
 
-def per_device(hidden_in, norm_gain, w_query, w_key, w_value, w_out, session_ids, block_anchor):
+def per_device_ring(hidden_in, norm_gain, w_query, w_key, w_value, w_out, session_ids, block_anchor):
     whole, gain_full = (
         lax.all_gather(hidden_in, "head", axis=1, tiled=True),
         lax.all_gather(norm_gain, "head", axis=0, tiled=True),
@@ -141,6 +141,67 @@
     return lax.psum_scatter(terms.astype(jnp.bfloat16), "head", scatter_dimension=1, tiled=True)
 
 
+def token_table(session_ids, block_anchor, owners_rows):
+    starts = session_starts(session_ids)
+    owner = jnp.arange(owners_rows, dtype=jnp.int32)
+    contiguous = jnp.take(block_anchor, owner // BLOCK) * BLOCK + owner % BLOCK
+    session = jnp.take(session_ids, contiguous)
+    position = contiguous - jnp.take(starts, contiguous)
+    return contiguous, session, position
+
+
+def transposed(block, n):
+    route = [(c * n + h, h * n + c) for c in range(n) for h in range(n)]
+    return lax.ppermute(block, ("ctx", "head"), route)
+
+
+def per_device_ws(hidden_in, norm_gain, w_query, w_key, w_value, w_out, session_ids, block_anchor):
+    n = lax.axis_size("ctx")
+    cycle_index = lax.axis_index("ctx")
+    tok_rows, local_feats = hidden_in.shape
+    wide = hidden_in.astype(jnp.float32)
+    squares = lax.psum(jnp.sum(wide * wide, axis=-1, keepdims=True), "head")
+    normed = (
+        wide
+        * lax.rsqrt(squares / (local_feats * n) + norm_epsilon)
+        * norm_gain.astype(jnp.float32)
+    ).astype(jnp.bfloat16)
+    every = lax.all_gather(transposed(normed, n), "head", axis=0, tiled=True)
+    q_cols, k_cols = w_query.shape[1], w_key.shape[1]
+    stacked = jnp.concatenate([w_query, w_key, w_value], axis=1)
+    partial = jnp.dot(every, stacked, preferred_element_type=jnp.float32)
+    mine = lax.psum_scatter(partial, "ctx", scatter_dimension=0, tiled=True)
+    kv_local = k_cols // HD
+    query_raw = mine[:, :q_cols].reshape(tok_rows, kv_local, GROUP, HD)
+    key_raw = mine[:, q_cols : q_cols + k_cols].reshape(tok_rows, kv_local, HD)
+    value_raw = mine[:, q_cols + k_cols :].reshape(tok_rows, kv_local, HD)
+    contiguous, session, position = token_table(session_ids, block_anchor, tok_rows * n)
+    my_pos = lax.dynamic_slice_in_dim(contiguous, cycle_index * tok_rows, tok_rows)
+    my_seg = lax.dynamic_slice_in_dim(session, cycle_index * tok_rows, tok_rows)
+    my_place = lax.dynamic_slice_in_dim(position, cycle_index * tok_rows, tok_rows)
+    query_heads = rotary(query_raw, my_place).astype(jnp.bfloat16)
+    key_heads = rotary(key_raw, my_place).astype(jnp.bfloat16)
+    value_heads = value_raw.astype(jnp.bfloat16)
+    kv_all = lax.all_gather(jnp.stack([key_heads, value_heads]), "ctx", axis=1, tiled=True)
+    scores = jnp.einsum(
+        "qagd,kad->qagk", query_heads, kv_all[0], preferred_element_type=jnp.float32
+    ) * (1.0 / math.sqrt(HD))
+    allowed = ((my_seg[:, None] == session[None, :]) & (contiguous[None, :] <= my_pos[:, None]))[
+        :, None, None, :
+    ]
+    row_max = jnp.max(jnp.where(allowed, scores, masked_score), axis=-1, keepdims=True)
+    weights = jnp.where(allowed, jnp.exp(scores - row_max), 0.0)
+    row_sum = jnp.sum(weights, axis=-1, keepdims=True)
+    mixed = jnp.einsum(
+        "qagk,kad->qagd", weights.astype(jnp.bfloat16), kv_all[1], preferred_element_type=jnp.float32
+    )
+    attended = (mixed / row_sum).astype(jnp.bfloat16).reshape(tok_rows, -1)
+    att_all = lax.all_gather(attended, "ctx", axis=0, tiled=True)
+    terms = jnp.dot(att_all, w_out, preferred_element_type=jnp.float32).astype(jnp.bfloat16)
+    summed = lax.psum_scatter(terms, "head", scatter_dimension=0, tiled=True)
+    return transposed(summed, n)
+
+
 def solution(mesh):
     in_specs = (
         P(("groups", "ctx"), "head"),
@@ -153,6 +214,8 @@
         P("groups"),
     )
     out_specs = P(("groups", "ctx"), "head")
+    square = mesh.shape["ctx"] == mesh.shape["head"]
+    per_device = per_device_ws if square else per_device_ring
     return jax.shard_map(
         per_device, mesh=mesh, in_specs=in_specs, out_specs=out_specs, check_vma=False
     )

time: 302 us -> 256 us (0.85)
  waiting for transfers between devices: 250 us -> 172 us
  blocking collectives: 5.31 us -> 21 us
  starting transfers between devices: 0.37 us -> 11.1 us
  local copies, waits for them, and re-layouts: 4.74 us -> 15.1 us
  matrix products: 16.6 us -> 12 us
    all_gather x5 -> x2, waiting for transfers between devices: 194 us -> 49.4 us  [the longest x1 29.4 us: per_device_ws(): att_all = lax.all_gather(attended, 'ctx', axis=0, tiled=True)]
    reduce_scatter x1 -> x2, waiting for transfers between devices: 28.5 us -> 74.3 us  [the longest x1 45 us: per_device_ws(): mine = lax.psum_scatter(partial, 'ctx', scatter_dimension=0, tiled=True)]
    ppermute x3 -> x2, waiting for transfers between devices: 24.2 us -> 48 us  [transposed(): return lax.ppermute(block, ('ctx', 'head'), route)]
    ppermute x3 -> x2, starting transfers between devices: 0.18 us -> 11 us  [transposed(): return lax.ppermute(block, ('ctx', 'head'), route)]
    all_gather x1, blocking collectives: 5.31 us -> 15.2 us  [per_device_ws(): lax.all_gather(jnp.stack([key_heads, value_heads]), 'ctx', axis=1, tiled=...]
    gather x5 -> x3, local copies, waits for them, and re-layouts: 3.47 us -> 9.73 us  [the longest x1 4.53 us: token_table(): session = jnp.take(session_ids, contiguous)]
    psum x0 -> x1, blocking collectives: none -> 5.77 us  [per_device_ws(): squares = lax.psum(jnp.sum(wide * wide, axis=-1, keepdims=True), 'head')]
    gather x4 -> x3, other arithmetic: 0.02 us -> 5.02 us  [the longest x2 4.36 us: token_table(): contiguous = jnp.take(block_anchor, owner // BLOCK) * BLOCK + owner % BLOCK]
  transfers between devices with their start and end apart: 9 -> 6, of which waited for: 9 -> 6; matrix products, arithmetic and copies ran while one was open for 8% -> 6% of each run, Pallas kernels for 0% -> 0%
where the time goes in v1:
time: 256 us
  waiting for transfers between devices  172 us (67%)
  blocking collectives  21 us (8%)
  local copies, waits for them, and re-layouts  15.1 us (6%)
  between operations  13.3 us (5%)
  matrix products  12 us (5%)
  other arithmetic  11.5 us (4%)
  starting transfers between devices  11.1 us (4%)
    ppermute x2, waiting for transfers between devices, transposed(): return lax.ppermute(block, ('ctx', 'head'), route)  48 us
    reduce_scatter x1, waiting for transfers between devices, per_device_ws(): mine = lax.psum_scatter(partial, 'ctx', scatter_dimension=0, tiled=True)  45 us
    all_gather x1, waiting for transfers between devices, per_device_ws(): att_all = lax.all_gather(attended, 'ctx', axis=0, tiled=True)  29.4 us
    reduce_scatter x1, waiting for transfers between devices, per_device_ws(): summed = lax.psum_scatter(terms, 'head', scatter_dimension=0, tiled=True)  29.3 us
    all_gather x1, waiting for transfers between devices, per_device_ws(): every = lax.all_gather(transposed(normed, n), 'head', axis=0, tiled=True)  20 us
    all_gather x1, blocking collectives, per_device_ws(): lax.all_gather(jnp.stack([key_heads, value_heads]), 'ctx', axis=1, tiled=...  15.2 us
    ppermute x2, starting transfers between devices, transposed(): return lax.ppermute(block, ('ctx', 'head'), route)  11 us
    psum x1, blocking collectives, per_device_ws(): squares = lax.psum(jnp.sum(wide * wide, axis=-1, keepdims=True), 'head')  5.77 us
  transfers between devices with their start and end apart: 6, of which 6 were waited for; matrix products, arithmetic and copies ran while one was open for 6% of the time, Pallas kernels for 0%

profile of v1, /device:TPU:2, one launch (start us, length us, event | category | flops | bytes accessed | tf_op | source)
XLA Modules:
  0.0 255.6 jit_solution(16360974636456427770)
XLA Ops:
  7.3 1.2 fusion.18
  8.5 5.8 %psum.7 = f32[256,1]{0,1:T(1,128)S(1)} all-reduce(f32[256,1]{0,1:T(1,128)S(1)} %bitcast.89), channel_id=1, replica_groups=mesh['groups'=2,'ctx'=4,'head'=4] {'head'}, use_global_device_ids=true, to_apply=%region_1.0 | all-reduce | flops 256 | bytes 2048 | tf_op jit(solution)/shard_map/psum | solution.py:163
  14.3 1.2 fusion.20
  15.5 5.6 %collective-permute-start = (bf16[256,1024]{1,0:T(8,128)(2,1)S(1)}, bf16[256,1024]{1,0:T(8,128)(2,1)S(1)}, u32[]{:S(2)}, u32[]{:S(2)}) collective-permute-start(bf16[256,1024]{1,0:T(8,128)(2,1)S(1)} %fusion.20), channel_id=1, source_target_pairs={{0,0},{1,4},{2,8},{3,12},{4,1},{5,5},{6,9},{7,13},{8,2},{9,6},{10,... | collective-permute-start | bytes 1572872 | tf_op jit(solution)/shard_map/ppermute | solution.py:155
  21.2 23.8 %collective-permute-done = bf16[256,1024]{1,0:T(8,128)(2,1)S(1)} collective-permute-done((bf16[256,1024]{1,0:T(8,128)(2,1)S(1)}, bf16[256,1024]{1,0:T(8,128)(2,1)S(1)}, u32[]{:S(2)}, u32[]{:S(2)}) %collective-permute-start) | collective-permute-done | bytes 524320 | tf_op jit(solution)/shard_map/ppermute | solution.py:155
  45.8 20.0 %all-gather.3.cloned.1.call-done = bf16[1024,1024]{1,0:T(8,128)(2,1)} async-done(((bf16[256,1024]{1,0:T(8,128)(2,1)}), bf16[1024,1024]{1,0:T(8,128)(2,1)}) %all-gather.3.cloned.1.call-update) | async-done | bytes 2097168 | tf_op jit(solution)/shard_map/all_gather | solution.py:169
  65.8 5.5 %fusion.9 = f32[1024,768]{1,0:T(8,128)} fusion(bf16[1024,1024]{1,0:T(8,128)(2,1)} %all-gather.3.cloned.1.call-done, bf16[1024,128]{1,0:T(8,128)(2,1)} %param.14, bf16[1024,128]{1,0:T(8,128)(2,1)} %param.13, bf16[1024,512]{1,0:T(8,128)(2,1)} %param.12), kind=kOutput, calls=%fused_computation.13 | convolution fusion | flops 1615331328 | bytes 6815744 | tf_op jit(solution)/shard_map/dot_general | solution.py:172
  72.6 4.3 %compare_select_fusion.1 = s32[1024,1]{0,1:T(1,128)S(1)} fusion(s32[]{:T(128)} %bitcast.4, s32[]{:T(128)} %bitcast.5, s32[]{:T(128)} %bitcast.6, s32[]{:T(128)} %bitcast.7, s32[]{:T(128)} %bitcast.8, s32[]{:T(128)} %bitcast.10, s32[]{:T(128)} %bitcast.9), kind=kLoop, calls=%fused_computation.58 | loop fusion | flops 23552 | bytes 4124 | tf_op jit(solution)/shard_map/jit(_take)/gather | solution.py:147
  77.6 4.5 %gather_fusion.1 = s32[1024]{0:T(1024)S(1)} fusion(s32[1024]{0:T(1024)S(1)} %copy-done.1, s32[1024]{0:T(1024)S(1)} %get-tuple-element.6), kind=kCustom, calls=%fused_computation.1.clone | custom fusion | bytes 12288 | tf_op jit(solution)/shard_map/jit(_take)/gather | solution.py:148
  82.4 4.5 %gather_fusion = s32[1024]{0:T(1024)S(1)} fusion(s32[1024]{0:T(1024)S(1)} %maximum_bitcast_fusion, s32[1024]{0:T(1024)S(1)} %get-tuple-element.6), kind=kCustom, calls=%fused_computation.clone | custom fusion | bytes 12288 | tf_op jit(solution)/shard_map/jit(_take)/gather | solution.py:149
  88.0 45.0 %reduce-scatter.3.cloned.1.call-done = f32[256,768]{1,0:T(8,128)} async-done(((f32[1024,768]{1,0:T(8,128)}), f32[256,768]{1,0:T(8,128)}) %reduce-scatter.3.cloned.1.call-update) | async-done | bytes 786448 | tf_op jit(solution)/shard_map/reduce_scatter | solution.py:173
  133.0 0.9 slice_bitcast_fusion.4
  134.5 0.9 fusion.41
  135.5 15.2 %all_gather.10 = bf16[2,1024,1,128]{3,1,2,0:T(8,128)(2,1)S(1)} all-gather(bf16[2,256,1,128]{3,1,2,0:T(8,128)(2,1)S(1)} %pad_maximum_fusion), channel_id=1, replica_groups=mesh['groups'=2,'ctx'=4,'head'=4] {'ctx'}, dimensions={1}, use_global_device_ids=true | all-gather | bytes 655360 | tf_op jit(solution)/shard_map/all_gather | solution.py:185
  150.8 1.1 slice.74
  152.5 0.9 fusion
  153.4 0.9 fusion.3
  154.3 1.7 fusion.24
  156.2 29.4 %all-gather.5.cloned.1.call-done = bf16[1024,512]{0,1:T(8,128)(2,1)} async-done(((bf16[256,512]{0,1:T(8,128)(2,1)}), bf16[1024,512]{0,1:T(8,128)(2,1)}) %all-gather.5.cloned.1.call-update) | async-done | bytes 1048592 | tf_op jit(solution)/shard_map/all_gather | solution.py:199
  185.6 3.9 %convolution_convert_fusion = bf16[1024,1024]{1,0:T(8,128)(2,1)} fusion(bf16[1024,512]{0,1:T(8,128)(2,1)} %all-gather.5.cloned.1.call-done, bf16[512,1024]{1,0:T(8,128)(2,1)S(1)} %copy-done), kind=kOutput, calls=%fused_computation.12 | convolution fusion | flops 1074790400 | bytes 4194304 | tf_op jit(solution)/shard_map/dot_general | solution.py:200
  189.4 29.3 %reduce-scatter.5.cloned.1.call-done = bf16[256,1024]{1,0:T(8,128)(2,1)} async-done(((bf16[1024,1024]{1,0:T(8,128)(2,1)}), bf16[256,1024]{1,0:T(8,128)(2,1)}) %reduce-scatter.5.cloned.1.call-update) | async-done | bytes 524304 | tf_op jit(solution)/shard_map/reduce_scatter | solution.py:201
  218.7 5.4 %collective-permute-start.1 = (bf16[256,1024]{1,0:T(8,128)(2,1)}, bf16[256,1024]{1,0:T(8,128)(2,1)S(1)}, u32[]{:S(2)}, u32[]{:S(2)}) collective-permute-start(bf16[256,1024]{1,0:T(8,128)(2,1)} %reduce-scatter.5.cloned.1.call-done), channel_id=1, source_target_pairs={{0,0},{1,4},{2,8},{3,12},{4,1},{5,5},{6,9},{7,13},{8,2},{9,6},{10,... | collective-permute-start | bytes 1572872 | tf_op jit(solution)/shard_map/ppermute | solution.py:155
  224.1 24.2 %collective-permute-done.1 = bf16[256,1024]{1,0:T(8,128)(2,1)S(1)} collective-permute-done((bf16[256,1024]{1,0:T(8,128)(2,1)}, bf16[256,1024]{1,0:T(8,128)(2,1)S(1)}, u32[]{:S(2)}, u32[]{:S(2)}) %collective-permute-start.1) | collective-permute-done | bytes 524320 | tf_op jit(solution)/shard_map/ppermute | solution.py:155
  248.3 0.8 copy.35
  (40 shorter events, 6.3 us)
Async XLA Ops:
  6.5 179.0 %copy-start = (bf16[512,1024]{1,0:T(8,128)(2,1)S(1)}, bf16[512,1024]{1,0:T(8,128)(2,1)}, u32[]{:S(2)}) copy-start(bf16[512,1024]{1,0:T(8,128)(2,1)} %param.15) | copy-start | bytes 3145732
  6.5 59.3 %all-gather.3.cloned.1.call-start = ((), (), s32[]{:S(2)}) async-start(), calls=%async_computation.2 | async-start | bytes 2621440 | tf_op jit(solution)/shard_map/all_gather | solution.py:169
  15.5 29.4 %collective-permute-start = (bf16[256,1024]{1,0:T(8,128)(2,1)S(1)}, bf16[256,1024]{1,0:T(8,128)(2,1)S(1)}, u32[]{:S(2)}, u32[]{:S(2)}) collective-permute-start(bf16[256,1024]{1,0:T(8,128)(2,1)S(1)} %fusion.20), channel_id=1, source_target_pairs={{0,0},{1,4},{2,8},{3,12},{4,1},{5,5},{6,9},{7,13},{8,2},{9,6},{10,... | collective-permute-start | bytes 1572872 | tf_op jit(solution)/shard_map/ppermute | solution.py:155
  45.0 0.8 copy-start.2
  45.8 25.6 %copy-start.1 = (s32[1024]{0:T(1024)S(1)}, s32[1024]{0:T(1024)}, u32[]{:S(2)}) copy-start(s32[1024]{0:T(1024)} %param.16) | copy-start | bytes 12292
  45.8 26.2 %copy-start.3 = (s32[8]{0:T(128)S(1)}, s32[8]{0:T(128)}, u32[]{:S(2)}) copy-start(s32[8]{0:T(128)} %param.17) | copy-start | bytes 100
  45.8 87.2 %reduce-scatter.3.cloned.1.call-start = ((), (), s32[]{:S(2)}) async-start(), calls=%async_computation.3 | async-start | bytes 3932160 | tf_op jit(solution)/shard_map/reduce_scatter | solution.py:173
  71.3 114.2 %all-gather.5.cloned.1.call-start = ((), (), s32[]{:S(2)}) async-start(), calls=%async_computation.4 | async-start | bytes 1310720 | tf_op jit(solution)/shard_map/all_gather | solution.py:199
  156.1 62.6 %reduce-scatter.5.cloned.1.call-start = ((), (), s32[]{:S(2)}) async-start(), calls=%async_computation.5 | async-start | bytes 2621440 | tf_op jit(solution)/shard_map/reduce_scatter | solution.py:201
  218.7 29.6 %collective-permute-start.1 = (bf16[256,1024]{1,0:T(8,128)(2,1)}, bf16[256,1024]{1,0:T(8,128)(2,1)S(1)}, u32[]{:S(2)}, u32[]{:S(2)}) collective-permute-start(bf16[256,1024]{1,0:T(8,128)(2,1)} %reduce-scatter.5.cloned.1.call-done), channel_id=1, source_target_pairs={{0,0},{1,4},{2,8},{3,12},{4,1},{5,5},{6,9},{7,13},{8,2},{9,6},{10,... | collective-permute-start | bytes 1572872 | tf_op jit(solution)/shard_map/ppermute | solution.py:155
Sparse Core Ops, SparseCore 0:
  45.9 19.8 all-gather.2
  71.4 61.5 reduce-scatter.2
  156.2 29.2 all-gather.4
  189.6 29.1 reduce-scatter.4

commit v2 on v1

--- a/solution.py
+++ b/solution.py
@@ -141,50 +141,106 @@
     return lax.psum_scatter(terms.astype(jnp.bfloat16), "head", scatter_dimension=1, tiled=True)
 
 
-def token_table(session_ids, block_anchor, owners_rows):
-    starts = session_starts(session_ids)
-    owner = jnp.arange(owners_rows, dtype=jnp.int32)
-    contiguous = jnp.take(block_anchor, owner // BLOCK) * BLOCK + owner % BLOCK
-    session = jnp.take(session_ids, contiguous)
-    position = contiguous - jnp.take(starts, contiguous)
+def token_table(session_ids, block_anchor):
+    offsets = jnp.arange(BLOCK, dtype=jnp.int32)
+    contiguous = (block_anchor[:, None] * BLOCK + offsets[None, :]).reshape(-1)
+    seg_table = session_ids.reshape(-1, BLOCK)
+    start_table = session_starts(session_ids).reshape(-1, BLOCK)
+    session = jnp.take(seg_table, block_anchor, axis=0).reshape(-1)
+    position = contiguous - jnp.take(start_table, block_anchor, axis=0).reshape(-1)
     return contiguous, session, position
 
 
 def transposed(block, n):
     route = [(c * n + h, h * n + c) for c in range(n) for h in range(n)]
     return lax.ppermute(block, ("ctx", "head"), route)
+
+
+def line_gather(block, axis, n):
+    me = lax.axis_index(axis)
+    parts = [block] + [passed_along(block, axis, d) for d in range(1, n)]
+    stacked = jnp.stack(parts)
+    source_slot = (me - jnp.arange(n, dtype=jnp.int32)) % n
+    return jnp.take(stacked, source_slot, axis=0).reshape((-1,) + block.shape[1:])
+
+
+def xor_swap(block, axis, n, d):
+    return lax.ppermute(block, axis, [(i, i ^ d) for i in range(n)])
+
+
+def halving_gather(block, axis, n):
+    me = lax.axis_index(axis)
+    offsets = [0]
+    held = block[None]
+    d = n // 2
+    while d >= 1:
+        held = jnp.concatenate([held, xor_swap(held, axis, n, d)])
+        offsets = offsets + [o ^ d for o in offsets]
+        d //= 2
+    slot_of = jnp.asarray([offsets.index(o) for o in range(n)], jnp.int32)
+    order = jnp.take(slot_of, me ^ jnp.arange(n, dtype=jnp.int32))
+    return jnp.take(held, order, axis=0).reshape((-1,) + block.shape[1:])
+
+
+def halving_scatter(block, axis, n):
+    me = lax.axis_index(axis)
+    rows = block.shape[0] // n
+    held = block.reshape((n, rows) + block.shape[1:])
+    total = None
+    d = 1
+    while d < n:
+        count = held.shape[0]
+        slots = jnp.arange(count // 2, dtype=jnp.int32)
+        mine_bit = (me // d) % 2
+        keep = jnp.take(held, slots * 2 + mine_bit, axis=0)
+        send = jnp.take(held, slots * 2 + 1 - mine_bit, axis=0)
+        if total is not None:
+            keep_sum = jnp.take(total, slots * 2 + mine_bit, axis=0)
+            send_sum = jnp.take(total, slots * 2 + 1 - mine_bit, axis=0)
+            keep = keep_sum
+            send = send_sum.astype(block.dtype)
+        total = keep.astype(jnp.float32) + xor_swap(send, axis, n, d).astype(jnp.float32)
+        held = total
+        d *= 2
+    return total[0].astype(block.dtype)
 
 
 def per_device_ws(hidden_in, norm_gain, w_query, w_key, w_value, w_out, session_ids, block_anchor):
     n = lax.axis_size("ctx")
     cycle_index = lax.axis_index("ctx")
     tok_rows, local_feats = hidden_in.shape
+    moved = transposed(hidden_in, n)
     wide = hidden_in.astype(jnp.float32)
-    squares = lax.psum(jnp.sum(wide * wide, axis=-1, keepdims=True), "head")
+    squares = lax.psum(jnp.sum(wide * wide, axis=-1), "head")
+    scale_rows = lax.rsqrt(squares / (local_feats * n) + norm_epsilon)
+    side = transposed(jnp.concatenate([scale_rows, norm_gain.astype(jnp.float32)]), n)
     normed = (
-        wide
-        * lax.rsqrt(squares / (local_feats * n) + norm_epsilon)
-        * norm_gain.astype(jnp.float32)
+        moved.astype(jnp.float32) * side[:tok_rows, None] * side[None, tok_rows:]
     ).astype(jnp.bfloat16)
-    every = lax.all_gather(transposed(normed, n), "head", axis=0, tiled=True)
+    every = halving_gather(normed, "head", n)
     q_cols, k_cols = w_query.shape[1], w_key.shape[1]
-    stacked = jnp.concatenate([w_query, w_key, w_value], axis=1)
-    partial = jnp.dot(every, stacked, preferred_element_type=jnp.float32)
-    mine = lax.psum_scatter(partial, "ctx", scatter_dimension=0, tiled=True)
     kv_local = k_cols // HD
-    query_raw = mine[:, :q_cols].reshape(tok_rows, kv_local, GROUP, HD)
-    key_raw = mine[:, q_cols : q_cols + k_cols].reshape(tok_rows, kv_local, HD)
-    value_raw = mine[:, q_cols + k_cols :].reshape(tok_rows, kv_local, HD)
-    contiguous, session, position = token_table(session_ids, block_anchor, tok_rows * n)
+    part_kv = jnp.dot(
+        every, jnp.concatenate([w_key, w_value], axis=1), preferred_element_type=jnp.float32
+    )
+    part_q = jnp.dot(every, w_query, preferred_element_type=jnp.float32)
+    mine_kv = lax.psum_scatter(part_kv, "ctx", scatter_dimension=0, tiled=True)
+    mine_q = lax.psum_scatter(part_q, "ctx", scatter_dimension=0, tiled=True)
+    contiguous, session, position = token_table(session_ids, block_anchor)
     my_pos = lax.dynamic_slice_in_dim(contiguous, cycle_index * tok_rows, tok_rows)
     my_seg = lax.dynamic_slice_in_dim(session, cycle_index * tok_rows, tok_rows)
     my_place = lax.dynamic_slice_in_dim(position, cycle_index * tok_rows, tok_rows)
-    query_heads = rotary(query_raw, my_place).astype(jnp.bfloat16)
-    key_heads = rotary(key_raw, my_place).astype(jnp.bfloat16)
-    value_heads = value_raw.astype(jnp.bfloat16)
-    kv_all = lax.all_gather(jnp.stack([key_heads, value_heads]), "ctx", axis=1, tiled=True)
+    key_heads = rotary(mine_kv[:, :k_cols].reshape(tok_rows, kv_local, HD), my_place)
+    kv_rows = jnp.concatenate(
+        [key_heads.astype(jnp.bfloat16).reshape(tok_rows, k_cols), mine_kv[:, k_cols:].astype(jnp.bfloat16)],
+        axis=1,
+    )
+    kv_all = line_gather(kv_rows, "ctx", n)
+    keys = kv_all[:, :k_cols].reshape(-1, kv_local, HD)
+    values = kv_all[:, k_cols:].reshape(-1, kv_local, HD)
+    query_heads = rotary(mine_q.reshape(tok_rows, kv_local, GROUP, HD), my_place).astype(jnp.bfloat16)
     scores = jnp.einsum(
-        "qagd,kad->qagk", query_heads, kv_all[0], preferred_element_type=jnp.float32
+        "qagd,kad->qagk", query_heads, keys, preferred_element_type=jnp.float32
     ) * (1.0 / math.sqrt(HD))
     allowed = ((my_seg[:, None] == session[None, :]) & (contiguous[None, :] <= my_pos[:, None]))[
         :, None, None, :
@@ -193,12 +249,12 @@
     weights = jnp.where(allowed, jnp.exp(scores - row_max), 0.0)
     row_sum = jnp.sum(weights, axis=-1, keepdims=True)
     mixed = jnp.einsum(
-        "qagk,kad->qagd", weights.astype(jnp.bfloat16), kv_all[1], preferred_element_type=jnp.float32
+        "qagk,kad->qagd", weights.astype(jnp.bfloat16), values, preferred_element_type=jnp.float32
     )
     attended = (mixed / row_sum).astype(jnp.bfloat16).reshape(tok_rows, -1)
-    att_all = lax.all_gather(attended, "ctx", axis=0, tiled=True)
+    att_all = line_gather(attended, "ctx", n)
     terms = jnp.dot(att_all, w_out, preferred_element_type=jnp.float32).astype(jnp.bfloat16)
-    summed = lax.psum_scatter(terms, "head", scatter_dimension=0, tiled=True)
+    summed = halving_scatter(terms, "head", n)
     return transposed(summed, n)
 
 
@@ -214,7 +270,8 @@
         P("groups"),
     )
     out_specs = P(("groups", "ctx"), "head")
-    square = mesh.shape["ctx"] == mesh.shape["head"]
+    n_head = mesh.shape["head"]
+    square = mesh.shape["ctx"] == n_head and n_head & (n_head - 1) == 0
     per_device = per_device_ws if square else per_device_ring
     return jax.shard_map(
         per_device, mesh=mesh, in_specs=in_specs, out_specs=out_specs, check_vma=False

time: 256 us -> 226 us (0.88); the launches traced: 256 us -> 222 us
  waiting for transfers between devices: 172 us -> 137 us
  starting transfers between devices: 11.1 us -> 25.9 us
  blocking collectives: 21 us -> 6.82 us
    ppermute x0 -> x10, waiting for transfers between devices: none -> 54.4 us  [the longest x6 29.3 us: passed_along(): return lax.ppermute(block, axis, route)]
    all_gather x2 -> x0, waiting for transfers between devices: 49.4 us -> none  [the longest x1 29.4 us: per_device_ws(): att_all = lax.all_gather(attended, 'ctx', axis=0, tiled=True)]
    reduce_scatter x2, waiting for transfers between devices: 74.3 us -> 48.1 us  [the longest x1 27.4 us: per_device_ws(): mine_q = lax.psum_scatter(part_q, 'ctx', scatter_dimension=0, tiled=True)]
    all_gather x1 -> x0, blocking collectives: 15.2 us -> none  [per_device_ws(): lax.all_gather(jnp.stack([key_heads, value_heads]), 'ctx', axis=1, tiled=...]
    ppermute x2 -> x3, waiting for transfers between devices: 48 us -> 34.5 us  [transposed(): return lax.ppermute(block, ('ctx', 'head'), route)]
    ppermute x0 -> x10, starting transfers between devices: none -> 10.7 us  [the longest x6 9.96 us: passed_along(): return lax.ppermute(block, axis, route)]
    gather x3 -> x6, other arithmetic: 5.02 us -> 0.04 us  [the longest x2 4.36 us: token_table(): contiguous = jnp.take(block_anchor, owner // BLOCK) * BLOCK + owner % BLOCK]
    ppermute x2 -> x3, starting transfers between devices: 11 us -> 15.1 us  [transposed(): return lax.ppermute(block, ('ctx', 'head'), route)]
  transfers between devices with their start and end apart: 6 -> 15, of which waited for: 6 -> 12; matrix products, arithmetic and copies ran while one was open for 6% -> 7% of each run, Pallas kernels for 0% -> 0%
where the time goes in v2:
time: 226 us; the launch traced here: 222 us
  waiting for transfers between devices  137 us (61%)
  starting transfers between devices  25.9 us (11%)
  local copies, waits for them, and re-layouts  16.6 us (7%)
  between operations  13.8 us (6%)
  other arithmetic  11.6 us (5%)
  matrix products  10.4 us (5%)
  blocking collectives  6.82 us (3%)
    ppermute x3, waiting for transfers between devices, transposed(): return lax.ppermute(block, ('ctx', 'head'), route)  34.5 us
    ppermute x6, waiting for transfers between devices, passed_along(): return lax.ppermute(block, axis, route)  29.3 us
    reduce_scatter x1, waiting for transfers between devices, per_device_ws(): mine_q = lax.psum_scatter(part_q, 'ctx', scatter_dimension=0, tiled=True)  27.4 us
    ppermute x4, waiting for transfers between devices, xor_swap(): return lax.ppermute(block, axis, [(i, i ^ d) for i in range(n)])  25.2 us
    reduce_scatter x1, waiting for transfers between devices, per_device_ws(): mine_kv = lax.psum_scatter(part_kv, 'ctx', scatter_dimension=0, tiled=True)  20.7 us
    ppermute x3, starting transfers between devices, transposed(): return lax.ppermute(block, ('ctx', 'head'), route)  15.1 us
    ppermute x6, starting transfers between devices, passed_along(): return lax.ppermute(block, axis, route)  9.96 us
    psum x1, blocking collectives, per_device_ws(): squares = lax.psum(jnp.sum(wide * wide, axis=-1), 'head')  6.82 us
  transfers between devices with their start and end apart: 15, of which 12 were waited for; matrix products, arithmetic and copies ran while one was open for 7% of the time, Pallas kernels for 0%

profile of v2, /device:TPU:2, one launch (start us, length us, event | category | flops | bytes accessed | tf_op | source)
XLA Modules:
  0.0 222.1 jit_solution(5215611325704222248)
XLA Ops:
  6.5 4.6 %collective-permute-start = (bf16[256,1024]{1,0:T(8,128)(2,1)}, bf16[256,1024]{1,0:T(8,128)(2,1)S(1)}, u32[]{:S(2)}, u32[]{:S(2)}) collective-permute-start(bf16[256,1024]{1,0:T(8,128)(2,1)} %param.15), channel_id=1, source_target_pairs={{0,0},{1,4},{2,8},{3,12},{4,1},{5,5},{6,9},{7,13},{8,2},{9,6},{10,... | collective-permute-start | bytes 1572872 | tf_op jit(solution)/shard_map/ppermute | solution.py:156
  13.0 6.8 %psum.7 = f32[256]{0:T(256)S(1)} all-reduce(f32[256]{0:T(256)S(1)} %multiply_reduce_fusion), channel_id=1, replica_groups=mesh['groups'=2,'ctx'=4,'head'=4] {'head'}, use_global_device_ids=true, to_apply=%region_1.0 | all-reduce | flops 256 | bytes 2048 | tf_op jit(solution)/shard_map/psum | solution.py:214
  19.9 3.6 %collective-permute-start.1 = (f32[1280]{0:T(1024)S(1)}, f32[1280]{0:T(1024)S(1)}, u32[]{:S(2)}, u32[]{:S(2)}) collective-permute-start(f32[1280]{0:T(1024)S(1)} %pad_maximum_fusion.5), channel_id=1, source_target_pairs={{0,0},{1,4},{2,8},{3,12},{4,1},{5,5},{6,9},{7,13},{8,2},{9,6},{10,... | collective-permute-start | bytes 15368 | tf_op jit(solution)/shard_map/ppermute | solution.py:156
  23.5 13.1 %collective-permute-done.1 = f32[1280]{0:T(1024)S(1)} collective-permute-done((f32[1280]{0:T(1024)S(1)}, f32[1280]{0:T(1024)S(1)}, u32[]{:S(2)}, u32[]{:S(2)}) %collective-permute-start.1) | collective-permute-done | bytes 5152 | tf_op jit(solution)/shard_map/ppermute | solution.py:156
  36.9 9.2 %collective-permute-done.2 = bf16[1,256,1024]{2,1,0:T(8,128)(2,1)S(1)} collective-permute-done((bf16[1,256,1024]{2,1,0:T(8,128)(2,1)S(1)}, bf16[1,256,1024]{2,1,0:T(8,128)(2,1)S(1)}, u32[]{:S(2)}, u32[]{:S(2)}) %collective-permute-start.2) | collective-permute-done | bytes 524320 | tf_op jit(solution)/shard_map/ppermute | solution.py:168
  47.0 2.0 collective-permute-done.3
  49.0 2.8 %pad_maximum_fusion = bf16[4,256,1024]{2,1,0:T(8,128)(2,1)} fusion(bf16[2,256,1024]{2,1,0:T(8,128)(2,1)} %collective-permute-done.3, bf16[1,256,1024]{2,1,0:T(8,128)(2,1)S(1)} %collective-permute-done.2, bf16[1,256,1024]{2,1,0:T(8,128)(2,1)S(1)} %fusion.19), kind=kLoop, calls=%fused_computation.16 | loop fusion | flops 2097152 | bytes 4194304 | tf_op jit(solution)/shard_map/concatenate | solution.py:177
  51.8 2.3 %gather_fusion.1 = bf16[4,256,1024]{2,1,0:T(8,128)(2,1)S(1)} fusion(bf16[4,256,1024]{2,1,0:T(8,128)(2,1)} %pad_maximum_fusion, s32[1024]{0:T(1024)S(1)} %pad_clamp_fusion.4), kind=kCustom, calls=%fused_computation.5 | custom fusion | bytes 4194320 | tf_op jit(solution)/shard_map/jit(_take)/gather | solution.py:182
  57.6 4.2 %fusion.51 = f32[1024,512]{1,0:T(8,128)} fusion(bf16[1024,1024]{1,0:T(8,128)(2,1)} %copy-done.2, bf16[1024,512]{1,0:T(8,128)(2,1)S(1)} %copy-done.4), kind=kOutput, calls=%fused_computation.122 | convolution fusion | flops 1073741824 | bytes 5242880 | tf_op jit(solution)/shard_map/dot_general | solution.py:226
  65.6 20.7 %reduce-scatter.3.cloned.1.call-done = f32[256,256]{1,0:T(8,128)} async-done(((f32[1024,256]{1,0:T(8,128)}), f32[256,256]{1,0:T(8,128)}) %reduce-scatter.3.cloned.1.call-update) | async-done | bytes 262160 | tf_op jit(solution)/shard_map/reduce_scatter | solution.py:227
  90.4 2.3 %collective-permute-start.6 = (bf16[256,256]{1,0:T(8,128)(2,1)S(1)}, bf16[256,256]{1,0:T(8,128)(2,1)S(1)}, u32[]{:S(2)}, u32[]{:S(2)}) collective-permute-start(bf16[256,256]{1,0:T(8,128)(2,1)S(1)} %pad_maximum_fusion.4), channel_id=1, source_target_pairs={{4,0},{8,4},{12,8},{0,12},{5,1},{9,5},{13,9},{1,13},{6,2},{10,6},{... | collective-permute-start | bytes 393224 | tf_op jit(solution)/shard_map/ppermute | solution.py:21
  93.0 4.2 %collective-permute-done.4 = bf16[256,256]{1,0:T(8,128)(2,1)S(1)} collective-permute-done((bf16[256,256]{1,0:T(8,128)(2,1)S(1)}, bf16[256,256]{1,0:T(8,128)(2,1)S(1)}, u32[]{:S(2)}, u32[]{:S(2)}) %collective-permute-start.4) | collective-permute-done | bytes 131104 | tf_op jit(solution)/shard_map/ppermute | solution.py:21
  97.2 9.8 %collective-permute-done.5 = bf16[256,256]{1,0:T(8,128)(2,1)S(1)} collective-permute-done((bf16[256,256]{1,0:T(8,128)(2,1)S(1)}, bf16[256,256]{1,0:T(8,128)(2,1)S(1)}, u32[]{:S(2)}, u32[]{:S(2)}) %collective-permute-start.5) | collective-permute-done | bytes 131104 | tf_op jit(solution)/shard_map/ppermute | solution.py:21
  107.8 27.4 %reduce-scatter.5.cloned.1.call-done = f32[256,512]{1,0:T(8,128)} async-done(((f32[1024,512]{1,0:T(8,128)}), f32[256,512]{1,0:T(8,128)}) %reduce-scatter.5.cloned.1.call-update) | async-done | bytes 524304 | tf_op jit(solution)/shard_map/reduce_scatter | solution.py:228
  139.9 3.4 %collective-permute-start.7 = (bf16[256,512]{1,0:T(8,128)(2,1)S(1)}, bf16[256,512]{1,0:T(8,128)(2,1)S(1)}, u32[]{:S(2)}, u32[]{:S(2)}) collective-permute-start(bf16[256,512]{1,0:T(8,128)(2,1)S(1)} %copy.22), channel_id=1, source_target_pairs={{12,0},{0,4},{4,8},{8,12},{13,1},{1,5},{5,9},{9,13},{14,2},{2,6},{... | collective-permute-start | bytes 786440 | tf_op jit(solution)/shard_map/ppermute | solution.py:21
  143.4 2.6 %collective-permute-start.9 = (bf16[256,512]{1,0:T(8,128)(2,1)S(1)}, bf16[256,512]{1,0:T(8,128)(2,1)S(1)}, u32[]{:S(2)}, u32[]{:S(2)}) collective-permute-start(bf16[256,512]{1,0:T(8,128)(2,1)S(1)} %copy.22), channel_id=1, source_target_pairs={{4,0},{8,4},{12,8},{0,12},{5,1},{9,5},{13,9},{1,13},{6,2},{10,6},{... | collective-permute-start | bytes 786440 | tf_op jit(solution)/shard_map/ppermute | solution.py:21
  146.2 4.9 %collective-permute-done.7 = bf16[256,512]{1,0:T(8,128)(2,1)S(1)} collective-permute-done((bf16[256,512]{1,0:T(8,128)(2,1)S(1)}, bf16[256,512]{1,0:T(8,128)(2,1)S(1)}, u32[]{:S(2)}, u32[]{:S(2)}) %collective-permute-start.7) | collective-permute-done | bytes 262176 | tf_op jit(solution)/shard_map/ppermute | solution.py:21
  151.1 10.4 %collective-permute-done.8 = bf16[256,512]{1,0:T(8,128)(2,1)S(1)} collective-permute-done((bf16[256,512]{1,0:T(8,128)(2,1)S(1)}, bf16[256,512]{1,0:T(8,128)(2,1)S(1)}, u32[]{:S(2)}, u32[]{:S(2)}) %collective-permute-start.8) | collective-permute-done | bytes 262176 | tf_op jit(solution)/shard_map/ppermute | solution.py:21
  162.5 2.6 %convolution_convert_fusion = bf16[1024,1024]{1,0:T(8,128)(2,1)} fusion(bf16[1024,512]{1,0:T(8,128)(2,1)S(1)} %bitcast_select_fusion.2, bf16[512,1024]{1,0:T(8,128)(2,1)S(1)} %copy-done), kind=kOutput, calls=%fused_computation.21 | convolution fusion | flops 1074790400 | bytes 4194304 | tf_op jit(solution)/shard_map/dot_general | solution.py:256
  165.1 2.2 gather_fusion.7
  168.5 2.2 gather_fusion.6
  172.6 13.4 %collective-permute-done.11 = bf16[1,256,1024]{2,1,0:T(8,128)(2,1)S(1)} collective-permute-done((bf16[1,256,1024]{2,1,0:T(8,128)(2,1)S(1)}, bf16[1,256,1024]{2,1,0:T(8,128)(2,1)S(1)}, u32[]{:S(2)}, u32[]{:S(2)}) %collective-permute-start.11) | collective-permute-done | bytes 524320 | tf_op jit(solution)/shard_map/ppermute | solution.py:168
  186.2 7.0 %collective-permute-start.12 = (bf16[256,1024]{1,0:T(8,128)(2,1)S(1)}, bf16[256,1024]{1,0:T(8,128)(2,1)S(1)}, u32[]{:S(2)}, u32[]{:S(2)}) collective-permute-start(bf16[256,1024]{1,0:T(8,128)(2,1)S(1)} %fusion.20), channel_id=1, source_target_pairs={{0,0},{1,4},{2,8},{3,12},{4,1},{5,5},{6,9},{7,13},{8,2},{9,6},{10,... | collective-permute-start | bytes 1572872 | tf_op jit(solution)/shard_map/ppermute | solution.py:156
  193.2 21.3 %collective-permute-done.12 = bf16[256,1024]{1,0:T(8,128)(2,1)S(1)} collective-permute-done((bf16[256,1024]{1,0:T(8,128)(2,1)S(1)}, bf16[256,1024]{1,0:T(8,128)(2,1)S(1)}, u32[]{:S(2)}, u32[]{:S(2)}) %collective-permute-start.12) | collective-permute-done | bytes 524320 | tf_op jit(solution)/shard_map/ppermute | solution.py:156
  (103 shorter events, 25.3 us)
Async XLA Ops:
  6.5 155.9 %copy-start = (bf16[512,1024]{1,0:T(8,128)(2,1)S(1)}, bf16[512,1024]{1,0:T(8,128)(2,1)}, u32[]{:S(2)}) copy-start(bf16[512,1024]{1,0:T(8,128)(2,1)} %param.20) | copy-start | bytes 3145732
  6.5 39.7 %copy-start.1 = (s32[4]{0:T(128)S(1)}, s32[4]{0:T(128)}, u32[]{:S(2)}) copy-start(s32[4]{0:T(128)} %constant.179.clone) | copy-start | bytes 52
  6.5 79.8 %reduce-scatter.3.cloned.1.call-start = ((), (), s32[]{:S(2)}) async-start(), calls=%async_computation.2 | async-start | bytes 1310720 | tf_op jit(solution)/shard_map/reduce_scatter | solution.py:227
  6.5 30.1 %collective-permute-start = (bf16[256,1024]{1,0:T(8,128)(2,1)}, bf16[256,1024]{1,0:T(8,128)(2,1)S(1)}, u32[]{:S(2)}, u32[]{:S(2)}) collective-permute-start(bf16[256,1024]{1,0:T(8,128)(2,1)} %param.15), channel_id=1, source_target_pairs={{0,0},{1,4},{2,8},{3,12},{4,1},{5,5},{6,9},{7,13},{8,2},{9,6},{10,... | collective-permute-start | bytes 1572872 | tf_op jit(solution)/shard_map/ppermute | solution.py:156
  19.9 16.7 %collective-permute-start.1 = (f32[1280]{0:T(1024)S(1)}, f32[1280]{0:T(1024)S(1)}, u32[]{:S(2)}, u32[]{:S(2)}) collective-permute-start(f32[1280]{0:T(1024)S(1)} %pad_maximum_fusion.5), channel_id=1, source_target_pairs={{0,0},{1,4},{2,8},{3,12},{4,1},{5,5},{6,9},{7,13},{8,2},{9,6},{10,... | collective-permute-start | bytes 15368 | tf_op jit(solution)/shard_map/ppermute | solution.py:156
  36.8 9.2 %collective-permute-start.2 = (bf16[1,256,1024]{2,1,0:T(8,128)(2,1)S(1)}, bf16[1,256,1024]{2,1,0:T(8,128)(2,1)S(1)}, u32[]{:S(2)}, u32[]{:S(2)}) collective-permute-start(bf16[1,256,1024]{2,1,0:T(8,128)(2,1)S(1)} %fusion.19), channel_id=1, source_target_pairs={{0,2},{1,3},{2,0},{3,1},{4,6},{5,7},{6,4},{7,5},{8,10},{9,11},{10,... | collective-permute-start | bytes 1572872 | tf_op jit(solution)/shard_map/ppermute | solution.py:168
  46.1 2.9 %collective-permute-start.3 = (bf16[2,256,1024]{2,1,0:T(8,128)(2,1)S(1)}, bf16[2,256,1024]{2,1,0:T(8,128)(2,1)}, u32[]{:S(2)}, u32[]{:S(2)}) collective-permute-start(bf16[2,256,1024]{2,1,0:T(8,128)(2,1)S(1)} %pad_maximum_fusion.1), channel_id=1, source_target_pairs={{0,1},{1,0},{2,3},{3,2},{4,5},{5,4},{6,7},{7,6},{8,9},{9,8},{10,11... | collective-permute-start | bytes 3145736 | tf_op jit(solution)/shard_map/ppermute | solution.py:168
  54.1 1.7 copy-start.5
  54.1 1.7 copy-start.6
  54.5 1.3 copy-start.2
  55.8 1.8 copy-start.4
  57.5 77.7 %reduce-scatter.5.cloned.1.call-start = ((), (), s32[]{:S(2)}) async-start(), calls=%async_computation.3 | async-start | bytes 2621440 | tf_op jit(solution)/shard_map/reduce_scatter | solution.py:228
  61.7 0.7 copy-start.3
  61.7 1.2 copy-start.7
  88.9 8.3 %collective-permute-start.4 = (bf16[256,256]{1,0:T(8,128)(2,1)S(1)}, bf16[256,256]{1,0:T(8,128)(2,1)S(1)}, u32[]{:S(2)}, u32[]{:S(2)}) collective-permute-start(bf16[256,256]{1,0:T(8,128)(2,1)S(1)} %pad_maximum_fusion.4), channel_id=1, source_target_pairs={{12,0},{0,4},{4,8},{8,12},{13,1},{1,5},{5,9},{9,13},{14,2},{2,6},{... | collective-permute-start | bytes 393224 | tf_op jit(solution)/shard_map/ppermute | solution.py:21
  89.0 18.0 %collective-permute-start.5 = (bf16[256,256]{1,0:T(8,128)(2,1)S(1)}, bf16[256,256]{1,0:T(8,128)(2,1)S(1)}, u32[]{:S(2)}, u32[]{:S(2)}) collective-permute-start(bf16[256,256]{1,0:T(8,128)(2,1)S(1)} %pad_maximum_fusion.4), channel_id=1, source_target_pairs={{8,0},{12,4},{0,8},{4,12},{9,1},{13,5},{1,9},{5,13},{10,2},{14,6},... | collective-permute-start | bytes 393224 | tf_op jit(solution)/shard_map/ppermute | solution.py:21
  90.4 16.5 %collective-permute-start.6 = (bf16[256,256]{1,0:T(8,128)(2,1)S(1)}, bf16[256,256]{1,0:T(8,128)(2,1)S(1)}, u32[]{:S(2)}, u32[]{:S(2)}) collective-permute-start(bf16[256,256]{1,0:T(8,128)(2,1)S(1)} %pad_maximum_fusion.4), channel_id=1, source_target_pairs={{4,0},{8,4},{12,8},{0,12},{5,1},{9,5},{13,9},{1,13},{6,2},{10,6},{... | collective-permute-start | bytes 393224 | tf_op jit(solution)/shard_map/ppermute | solution.py:21
  139.9 11.2 %collective-permute-start.7 = (bf16[256,512]{1,0:T(8,128)(2,1)S(1)}, bf16[256,512]{1,0:T(8,128)(2,1)S(1)}, u32[]{:S(2)}, u32[]{:S(2)}) collective-permute-start(bf16[256,512]{1,0:T(8,128)(2,1)S(1)} %copy.22), channel_id=1, source_target_pairs={{12,0},{0,4},{4,8},{8,12},{13,1},{1,5},{5,9},{9,13},{14,2},{2,6},{... | collective-permute-start | bytes 786440 | tf_op jit(solution)/shard_map/ppermute | solution.py:21
  143.3 18.1 %collective-permute-start.8 = (bf16[256,512]{1,0:T(8,128)(2,1)S(1)}, bf16[256,512]{1,0:T(8,128)(2,1)S(1)}, u32[]{:S(2)}, u32[]{:S(2)}) collective-permute-start(bf16[256,512]{1,0:T(8,128)(2,1)S(1)} %copy.22), channel_id=1, source_target_pairs={{8,0},{12,4},{0,8},{4,12},{9,1},{13,5},{1,9},{5,13},{10,2},{14,6},... | collective-permute-start | bytes 786440 | tf_op jit(solution)/shard_map/ppermute | solution.py:21
  143.4 18.1 %collective-permute-start.9 = (bf16[256,512]{1,0:T(8,128)(2,1)S(1)}, bf16[256,512]{1,0:T(8,128)(2,1)S(1)}, u32[]{:S(2)}, u32[]{:S(2)}) collective-permute-start(bf16[256,512]{1,0:T(8,128)(2,1)S(1)} %copy.22), channel_id=1, source_target_pairs={{4,0},{8,4},{12,8},{0,12},{5,1},{9,5},{13,9},{1,13},{6,2},{10,6},{... | collective-permute-start | bytes 786440 | tf_op jit(solution)/shard_map/ppermute | solution.py:21
  168.4 2.9 %collective-permute-start.10 = (bf16[2,256,1024]{2,1,0:T(8,128)(2,1)}, bf16[2,256,1024]{2,1,0:T(8,128)(2,1)S(1)}, u32[]{:S(2)}, u32[]{:S(2)}) collective-permute-start(bf16[2,256,1024]{2,1,0:T(8,128)(2,1)} %broadcast_select_fusion), channel_id=1, source_target_pairs={{0,1},{1,0},{2,3},{3,2},{4,5},{5,4},{6,7},{7,6},{8,9},{9,8},{10,11... | collective-permute-start | bytes 3145736 | tf_op jit(solution)/shard_map/ppermute | solution.py:168
  172.0 14.0 %collective-permute-start.11 = (bf16[1,256,1024]{2,1,0:T(8,128)(2,1)S(1)}, bf16[1,256,1024]{2,1,0:T(8,128)(2,1)S(1)}, u32[]{:S(2)}, u32[]{:S(2)}) collective-permute-start(bf16[1,256,1024]{2,1,0:T(8,128)(2,1)S(1)} %select_convert_fusion), channel_id=1, source_target_pairs={{0,2},{1,3},{2,0},{3,1},{4,6},{5,7},{6,4},{7,5},{8,10},{9,11},{10,... | collective-permute-start | bytes 1572872 | tf_op jit(solution)/shard_map/ppermute | solution.py:168
  186.2 28.3 %collective-permute-start.12 = (bf16[256,1024]{1,0:T(8,128)(2,1)S(1)}, bf16[256,1024]{1,0:T(8,128)(2,1)S(1)}, u32[]{:S(2)}, u32[]{:S(2)}) collective-permute-start(bf16[256,1024]{1,0:T(8,128)(2,1)S(1)} %fusion.20), channel_id=1, source_target_pairs={{0,0},{1,4},{2,8},{3,12},{4,1},{5,5},{6,9},{7,13},{8,2},{9,6},{10,... | collective-permute-start | bytes 1572872 | tf_op jit(solution)/shard_map/ppermute | solution.py:156
Sparse Core Ops, SparseCore 0:
  57.6 28.7 reduce-scatter.2
  88.7 46.5 reduce-scatter.4
